TPU v7x, 256 devices: a whole 4x4x8 slice. The times are simulated.
256 devices in a mesh: snap: 4 (over x), line: 64 (over z, y, core).
Axes of the slice: x: 4, y: 4, z: 8, core: 2. Of those that a mesh axis runs over, the one named last changes fastest.
Arguments:
- ptdf_rows: float32 [8192, 20480], P('line'), may hold values from -4 to 4
- plan: float32 [5120, 2048], P(('snap', 'line')), may hold values from 0 to 0.15
- unit_bus: int32 [5120], replicated, may hold values from 0 to 20479
- min_up: int32 [5120], P(('snap', 'line')), may hold values from 1 to 24, as said below
- ramp_lag: int32 [5120], P(('snap', 'line')), may hold values from 1 to 6, as said below
- load_share: float32 [20480], replicated, may hold values from 0.004 to 0.04
- system_load: float32 [2048], P('snap'), may hold values from 0.6 to 1.4
- corridor_order: int32 [4], replicated, may hold values from 0 to 3, each once
- corridor_buses: int32 [4, 2], replicated, may hold values from 0 to 20479, as said below
- corridor_owner: int32 [4], replicated, may hold values from 0 to 63
- corridor_row: int32 [4], replicated, may hold values from 0 to 127
- corridor_ratio: float32 [4], replicated, may hold values from 0.5 to 2
Outputs:
- flows: float32 [8192, 2048], P('line', 'snap')
- corridor_sens: float32 [4, 20480], replicated
Inputs may be any that keep to these rules, and one draw needn't show every extreme that they name: `min_up`: some unit has a window of exactly 24. `ramp_lag`: some unit has a lag of exactly 6. `corridor_buses`: the two buses of a corridor differ.
All inputs are finite; a program needn't handle non-finite values.
Results may differ from a plain program's by a relative error of at most 0.000098.
Values sent between devices are 32-bit elements; how exact they have to be, the bound alone decides.
No kernel may reach another device: no remote copies, remote signals or barrier semaphores. Data moves between devices by JAX's collectives and lax.ppermute only.
A program may use at most 128 MiB of HBM per device.

v0:
```python
import jax
import jax.numpy as jnp
from jax import lax
from jax.sharding import Mesh
from jax.sharding import PartitionSpec as P

WMAX = 24
NC = 4
LINE = ("line_0", "line_1", "line_2")
SNAP_LINE = ("snap", "line_0", "line_1", "line_2")
ramp_gain = 0.5


def body(
    ptdf_rows,
    plan,
    unit_bus,
    min_up,
    ramp_lag,
    load_share,
    system_load,
    corridor_order,
    corridor_buses,
    corridor_owner,
    corridor_row,
    corridor_ratio,
):
    unit_count, horizon = plan.shape
    snap_count = lax.axis_size("snap")
    line_count = lax.axis_size(LINE)
    here = lax.axis_index(LINE)
    picked_rows = []
    for step in range(NC):
        chosen = corridor_order[step]
        row = lax.dynamic_index_in_dim(ptdf_rows, corridor_row[chosen], 0, keepdims=False)
        picked_rows.append(jnp.where(corridor_owner[chosen] == here, row, 0.0))
    all_rows = lax.psum(jnp.stack(picked_rows), LINE)
    padded = jnp.pad(plan, ((0, 0), (WMAX, 0)))
    inverse = 1.0 / min_up.astype(jnp.float32)
    held_mean = jnp.zeros(plan.shape, jnp.float32)
    lagged = jnp.zeros(plan.shape, jnp.float32)
    for offset in range(WMAX):
        shifted = padded[:, WMAX - offset : WMAX - offset + horizon]
        held_mean = held_mean + shifted * jnp.where(offset < min_up, inverse, 0.0)[:, None]
        lagged = lagged + shifted * (ramp_lag == offset).astype(jnp.float32)[:, None]
    dispatch = held_mean + ramp_gain * (plan - lagged)
    unit_blocks = lax.all_to_all(dispatch, "snap", split_axis=1, concat_axis=0, tiled=True)
    everyone = lax.all_gather(unit_blocks, LINE, axis=0, tiled=True)
    order_ids = unit_bus.reshape(snap_count, line_count, unit_count).transpose(1, 0, 2).reshape(-1)
    columns = jnp.concatenate(
        [jnp.take(ptdf_rows, order_ids, axis=1), jnp.take(all_rows, order_ids, axis=1)], axis=0
    )
    load_flows = jnp.dot(
        ptdf_rows, load_share, preferred_element_type=jnp.float32, precision=lax.Precision.HIGHEST
    )
    row_load_flows = jnp.dot(
        all_rows, load_share, preferred_element_type=jnp.float32, precision=lax.Precision.HIGHEST
    )
    sens_list = []
    weights = []
    row_coeff_list = []
    ends_list = []
    for step in range(NC):
        chosen = corridor_order[step]
        bus_from = corridor_buses[chosen, 0]
        bus_to = corridor_buses[chosen, 1]
        ratio = corridor_ratio[chosen]
        initial = all_rows[step]
        row_coeffs = []
        for prior in range(step):
            prior_from, prior_to = ends_list[prior]
            value = initial[prior_from] - initial[prior_to]
            for earlier in range(prior):
                value = value - row_coeffs[earlier] * (
                    sens_list[earlier][prior_from] - sens_list[earlier][prior_to]
                )
            row_coeffs.append(value)
        current = initial
        for prior in range(step):
            current = current - row_coeffs[prior] * sens_list[prior]
        weight = ratio / (1.0 + ratio * jnp.abs(current[bus_from] - current[bus_to]))
        sens_list.append(weight * current)
        weights.append(weight)
        row_coeff_list.append(row_coeffs)
        ends_list.append((bus_from, bus_to))
    coeff_list = []
    for step in range(NC):
        bus_from, bus_to = ends_list[step]
        coefficient = ptdf_rows[:, bus_from] - ptdf_rows[:, bus_to]
        for prior in range(step):
            coefficient = coefficient - coeff_list[prior] * (
                sens_list[prior][bus_from] - sens_list[prior][bus_to]
            )
        coeff_list.append(coefficient)
    flows_all = jnp.dot(
        columns, everyone, preferred_element_type=jnp.float32, precision=lax.Precision.HIGHEST
    )
    lines_here = ptdf_rows.shape[0]
    base = flows_all[:lines_here] - load_flows[:, None] * system_load[None, :]
    row_base = flows_all[lines_here:] - row_load_flows[:, None] * system_load[None, :]
    shift_list = []
    for step in range(NC):
        line_flow = row_base[step]
        for prior in range(step):
            line_flow = line_flow - row_coeff_list[step][prior] * shift_list[prior]
        shift_list.append(weights[step] * line_flow)
    flows = base
    for step in range(NC):
        flows = flows - coeff_list[step][:, None] * shift_list[step][None, :]
    return (flows, jnp.stack(sens_list))


def solution(mesh):
    torus = Mesh(
        mesh.devices.reshape(mesh.shape["snap"], 8, 4, 2), ("snap", "line_0", "line_1", "line_2")
    )
    in_specs = (
        P(LINE, None),
        P(SNAP_LINE, None),
        P(),
        P(SNAP_LINE),
        P(SNAP_LINE),
        P(),
        P("snap"),
        P(),
        P(),
        P(),
        P(),
        P(),
    )
    out_specs = (P(LINE, "snap"), P())
    return jax.shard_map(body, mesh=torus, in_specs=in_specs, out_specs=out_specs, check_vma=False)
```

profile of v0, /device:TPU:1, one launch (start us, length us, event | category | flops | bytes accessed | tf_op | source)
XLA Modules:
  0.0 346.1 jit_solution(17711845217591911878)
XLA Ops:
  7.9 0.7 compare_select_fusion.25
  9.3 6.7 %multiply_add_fusion = f32[20,2048]{1,0:T(8,128)S(1)} fusion(f32[20,2048]{1,0:T(8,128)} %param.13, f32[20]{0:T(128)S(1)} %get-tuple-element.133, f32[20]{0:T(128)S(1)} %get-tuple-element.134, f32[20]{0:T(128)S(1)} %get-tuple-element.112, f32[20]{0:T(128)S(1)} %get-tuple-element.113, f32[20]{0:T(128)S(1)} %get-tuple-element.114, ...), kind=kLoop, calls=%fused_computation.17 | loop fusion | flops 3973120 | bytes 331520 | tf_op jit(solution)/shard_map/add | solution.py:46
  16.1 0.7 copy.43
  16.8 4.8 %all-to-all-start = ((f32[20,4,512]{2,0,1:T(8,128)}), f32[20,4,512]{2,0,1:T(8,128)S(1)}, u32[]{:S(2)}, u32[]{:S(2)}) async-start(f32[20,4,512]{2,0,1:T(8,128)} %copy.43), calls=%async_computation | async-start | bytes 393216 | tf_op jit(solution)/shard_map/all_to_all | solution.py:47
  21.7 1.5 fusion.22
  30.9 1.5 fusion.20
  42.7 2.0 broadcast_select_fusion.3
  44.7 1.0 pad_maximum_fusion
  46.0 0.9 reshape.180
  47.3 11.8 %copy.41 = f32[128,20480]{0,1:T(8,128)} copy(f32[128,20480]{1,0:T(8,128)} %param.12) | data formatting | bytes 20971520 | tf_op args[0]
  59.1 21.6 %gather_fusion = f32[5120,128]{1,0:T(8,128)} fusion(f32[128,20480]{0,1:T(8,128)} %copy.41, s32[5120]{0:T(1024)S(1)} %broadcast_clamp_fusion), kind=kCustom, calls=%fused_computation | custom fusion | bytes 5263360 | tf_op jit(solution)/shard_map/jit(_take)/gather | solution.py:51
  80.8 4.2 %select_bitcast_fusion.1 = f32[128,5120]{0,1:T(8,128)S(1)} fusion(f32[5120,128]{1,0:T(8,128)} %gather_fusion, pred[5120]{0:T(1024)(128)(4,1)S(1)} %compare_and_fusion), kind=kLoop, calls=%fused_computation.7 | loop fusion | flops 655360 | bytes 5248000 | tf_op jit(solution)/shard_map/jit(_take)/select_n | solution.py:51
  85.0 10.8 %convolution_bitcast_fusion.1 = f32[128]{0:T(128)S(1)} fusion(f32[128,20480]{1,0:T(8,128)} %param.12, f32[20480,1]{0,1:T(1,128)S(1)} %bitcast.62), kind=kOutput, calls=%fused_computation.9 | convolution fusion | flops 31457280 | bytes 10568192 | tf_op jit(solution)/shard_map/dot_general | solution.py:53
  113.3 116.0 %all-reduce.3.cloned.1.call-done = f32[4,20480]{1,0:T(4,128)} async-done(((f32[4,20480]{1,0:T(4,128)}), f32[4,20480]{1,0:T(4,128)}) %all-reduce.3.cloned.1.call-update) | async-done | bytes 327696 | tf_op jit(solution)/shard_map/psum | solution.py:37
  229.4 6.5 %copy.42 = f32[4,20480]{0,1:T(8,128)} copy(f32[4,20480]{1,0:T(4,128)} %all-reduce.3.cloned.1.call-done) | data formatting | bytes 655360 | tf_op jit(solution)/shard_map/psum | solution.py:37
  235.9 21.6 %gather_fusion.1 = f32[5120,4]{1,0:T(8,128)} fusion(f32[4,20480]{0,1:T(8,128)} %copy.42, s32[5120]{0:T(1024)S(1)} %broadcast_clamp_fusion), kind=kCustom, calls=%fused_computation.1 | custom fusion | bytes 184320 | tf_op jit(solution)/shard_map/jit(_take)/gather | solution.py:51
  290.2 1.1 multiply_subtract_fusion.4
  291.3 1.2 fusion.8
  292.5 1.5 convolution_bitcast_fusion
  294.0 5.4 %select_bitcast_fusion = f32[4,5120]{0,1:T(8,128)} fusion(f32[5120,4]{1,0:T(8,128)} %gather_fusion.1, pred[5120]{0:T(1024)(128)(4,1)S(1)} %compare_and_fusion), kind=kLoop, calls=%fused_computation.6 | loop fusion | flops 20480 | bytes 168960 | tf_op jit(solution)/shard_map/jit(_take)/select_n | solution.py:51
  299.5 1.0 pad_maximum_fusion.1
  300.5 17.4 %all-gather.2.cloned.1.call-done = f32[5120,512]{1,0:T(8,128)} async-done(((f32[80,512]{1,0:T(8,128)}), f32[5120,512]{1,0:T(8,128)}) %all-gather.2.cloned.1.call-update) | async-done | bytes 10485776 | tf_op jit(solution)/shard_map/all_gather | solution.py:48
  317.9 20.4 %fusion = f32[132,512]{1,0:T(8,128)S(1)} fusion(f32[5120,512]{1,0:T(8,128)} %all-gather.2.cloned.1.call-done, f32[4,5120]{0,1:T(8,128)} %select_bitcast_fusion, f32[128,5120]{0,1:T(8,128)S(1)} %select_bitcast_fusion.1), kind=kOutput, calls=%fused_computation.2 | convolution fusion | flops 4153036800 | bytes 13459456 | tf_op jit(solution)/shard_map/dot_general | solution.py:95
  338.4 0.9 fusion.7
  (44 shorter events, 11.9 us)
Async XLA Ops:
  7.2 77.9 %copy-start = (f32[20480]{0:T(1024)S(1)}, f32[20480]{0:T(1024)}, u32[]{:S(2)}) copy-start(f32[20480]{0:T(1024)} %param.17) | copy-start | bytes 245764
  16.8 95.8 %all-to-all-start = ((f32[20,4,512]{2,0,1:T(8,128)}), f32[20,4,512]{2,0,1:T(8,128)S(1)}, u32[]{:S(2)}, u32[]{:S(2)}) async-start(f32[20,4,512]{2,0,1:T(8,128)} %copy.43), calls=%async_computation | async-start | bytes 393216 | tf_op jit(solution)/shard_map/all_to_all | solution.py:47
  21.7 207.7 %all-reduce.3.cloned.1.call-start = ((), (), s32[]{:S(2)}) async-start(), calls=%async_computation.1 | async-start | bytes 655360 | tf_op jit(solution)/shard_map/psum | solution.py:37
  45.8 272.2 %all-gather.2.cloned.1.call-start = ((), (), s32[]{:S(2)}) async-start(), calls=%async_computation.2 | async-start | bytes 10649600 | tf_op jit(solution)/shard_map/all_gather | solution.py:48
  85.0 10.8 %copy-start.2 = (s32[4,2]{0,1:T(2,128)S(1)}, s32[4,2]{0,1:T(2,128)}, u32[]{:S(2)}) copy-start(s32[4,2]{0,1:T(2,128)} %param.20) | copy-start | bytes 100
  85.0 26.9 %copy-start.4 = (f32[4]{0:T(128)S(1)}, f32[4]{0:T(128)}, u32[]{:S(2)}) copy-start(f32[4]{0:T(128)} %param.23) | copy-start | bytes 52
  229.3 28.2 %copy-start.1 = (f32[4,20480]{1,0:T(4,128)S(1)}, f32[4,20480]{1,0:T(4,128)}, u32[]{:S(2)}) copy-start(f32[4,20480]{1,0:T(4,128)} %all-reduce.3.cloned.1.call-done) | copy-start | bytes 983044
  300.5 37.8 %copy-start.3 = (f32[512]{0:T(512)S(1)}, f32[512]{0:T(512)}, u32[]{:S(2)}) copy-start(f32[512]{0:T(512)} %param.18) | copy-start | bytes 6148
Sparse Core Ops, SparseCore 0:
  45.9 183.4 all-reduce.2
  232.7 85.2 all-gather.1
where the time goes:
time: 348 us; the launch traced here: 346 us
  waiting for transfers between devices  133 us (38%)
  local copies, waits for them, and re-layouts  75.6 us (22%)
  between operations  72.9 us (21%)
  matrix products  32.7 us (9%)
  other arithmetic  26.4 us (8%)
  starting transfers between devices  5.06 us (1%)
    psum x1, waiting for transfers between devices, body(): all_rows = lax.psum(jnp.stack(picked_rows), LINE)  116 us
    gather x1, local copies, waits for them, and re-layouts, body(): jnp.take(ptdf_rows, order_ids, axis=1)  21.6 us
    gather x1, local copies, waits for them, and re-layouts, body(): jnp.take(all_rows, order_ids, axis=1)  21.6 us
    dot_general x1, matrix products, body(): jnp.dot(columns, everyone, preferred_element_type=jnp.float32, precision=...  20.4 us
    all_gather x1, waiting for transfers between devices, body(): everyone = lax.all_gather(unit_blocks, LINE, axis=0, tiled=True)  17.4 us
    unnamed x11, local copies, waits for them, and re-layouts  11.8 us
    dot_general x1, matrix products, body(): jnp.dot(ptdf_rows, load_share, preferred_element_type=jnp.float32, precis...  10.8 us
  transfers between devices with their start and end apart: 3, of which 2 were waited for; matrix products, arithmetic and copies ran while one was open for 30% of the time, Pallas kernels for 0%

commit v1 on v0

--- a/solution.py
+++ b/solution.py
@@ -34,7 +34,7 @@
         chosen = corridor_order[step]
         row = lax.dynamic_index_in_dim(ptdf_rows, corridor_row[chosen], 0, keepdims=False)
         picked_rows.append(jnp.where(corridor_owner[chosen] == here, row, 0.0))
-    all_rows = lax.psum(jnp.stack(picked_rows), LINE)
+    all_rows = jnp.sum(lax.all_gather(jnp.stack(picked_rows), LINE), axis=0)
     padded = jnp.pad(plan, ((0, 0), (WMAX, 0)))
     inverse = 1.0 / min_up.astype(jnp.float32)
     held_mean = jnp.zeros(plan.shape, jnp.float32)

time: 348 us -> 266 us (0.76)
  waiting for transfers between devices: 133 us -> 43.8 us
  other arithmetic: 26.4 us -> 36.4 us
    psum x1 -> x0, waiting for transfers between devices: 116 us -> none  [body(): all_rows = lax.psum(jnp.stack(picked_rows), LINE)]
    all_gather x0 -> x1, waiting for transfers between devices: none -> 33.6 us  [body(): all_rows = jnp.sum(lax.all_gather(jnp.stack(picked_rows), LINE), axis=0)]
    reduce_sum x0 -> x1, other arithmetic: none -> 10.8 us  [body(): all_rows = jnp.sum(lax.all_gather(jnp.stack(picked_rows), LINE), axis=0)]
    all_gather x1, waiting for transfers between devices: 17.4 us -> 10.1 us  [body(): everyone = lax.all_gather(unit_blocks, LINE, axis=0, tiled=True)]
    psum x1 -> x0, local copies, waits for them, and re-layouts: 6.55 us -> none  [body(): all_rows = lax.psum(jnp.stack(picked_rows), LINE)]
    reduce_sum x0 -> x1, local copies, waits for them, and re-layouts: none -> 5.56 us  [body(): all_rows = jnp.sum(lax.all_gather(jnp.stack(picked_rows), LINE), axis=0)]
    unnamed x11 -> x9, local copies, waits for them, and re-layouts: 11.8 us -> 11.9 us
  transfers between devices with their start and end apart: 3 -> 3, of which waited for: 2 -> 2; matrix products, arithmetic and copies ran while one was open for 30% -> 43% of each run, Pallas kernels for 0% -> 0%
where the time goes in v1:
time: 266 us; the launch traced here: 265 us
  local copies, waits for them, and re-layouts  74.8 us (28%)
  between operations  72.1 us (27%)
  waiting for transfers between devices  43.8 us (16%)
  other arithmetic  36.4 us (14%)
  matrix products  32.7 us (12%)
  starting transfers between devices  4.87 us (2%)
    all_gather x1, waiting for transfers between devices, body(): all_rows = jnp.sum(lax.all_gather(jnp.stack(picked_rows), LINE), axis=0)  33.6 us
    gather x1, local copies, waits for them, and re-layouts, body(): jnp.take(ptdf_rows, order_ids, axis=1)  21.9 us
    gather x1, local copies, waits for them, and re-layouts, body(): jnp.take(all_rows, order_ids, axis=1)  21.7 us
    dot_general x1, matrix products, body(): jnp.dot(columns, everyone, preferred_element_type=jnp.float32, precision=...  20.4 us
    unnamed x9, local copies, waits for them, and re-layouts  11.9 us
    reduce_sum x1, other arithmetic, body(): all_rows = jnp.sum(lax.all_gather(jnp.stack(picked_rows), LINE), axis=0)  10.8 us
    dot_general x1, matrix products, body(): jnp.dot(ptdf_rows, load_share, preferred_element_type=jnp.float32, precis...  10.8 us
    all_gather x1, waiting for transfers between devices, body(): everyone = lax.all_gather(unit_blocks, LINE, axis=0, tiled=True)  10.1 us
  transfers between devices with their start and end apart: 3, of which 2 were waited for; matrix products, arithmetic and copies ran while one was open for 43% of the time, Pallas kernels for 0%

profile of v1, /device:TPU:1, one launch (start us, length us, event | category | flops | bytes accessed | tf_op | source)
XLA Modules:
  0.0 264.6 jit_solution(300140139826508860)
XLA Ops:
  7.2 1.5 fusion.22
  16.3 1.5 fusion.20
  28.0 2.0 broadcast_select_fusion.3
  30.0 1.0 maximum_bitcast_fusion
  31.1 0.7 compare_select_fusion.25
  33.1 5.9 %multiply_add_fusion = f32[20,2048]{1,0:T(8,128)S(1)} fusion(f32[20,2048]{1,0:T(8,128)} %param.13, f32[20]{0:T(128)S(1)} %get-tuple-element.133, f32[20]{0:T(128)S(1)} %get-tuple-element.134, f32[20]{0:T(128)S(1)} %get-tuple-element.112, f32[20]{0:T(128)S(1)} %get-tuple-element.113, f32[20]{0:T(128)S(1)} %get-tuple-element.114, ...), kind=kLoop, calls=%fused_computation.17 | loop fusion | flops 3973120 | bytes 331520 | tf_op jit(solution)/shard_map/add | solution.py:46
  39.9 4.8 %all-to-all-start = ((f32[20,4,512]{2,0,1:T(8,128)}), f32[20,4,512]{2,0,1:T(8,128)S(1)}, u32[]{:S(2)}, u32[]{:S(2)}) async-start(f32[20,4,512]{2,0,1:T(8,128)} %copy.25), calls=%async_computation | async-start | bytes 393216 | tf_op jit(solution)/shard_map/all_to_all | solution.py:47
  44.7 0.9 reshape.180
  46.0 11.9 %copy.23 = f32[128,20480]{0,1:T(8,128)} copy(f32[128,20480]{1,0:T(8,128)} %param.12) | data formatting | bytes 20971520 | tf_op args[0]
  57.9 21.9 %gather_fusion = f32[5120,128]{1,0:T(8,128)} fusion(f32[128,20480]{0,1:T(8,128)} %copy.23, s32[5120]{0:T(1024)S(1)} %broadcast_clamp_fusion), kind=kCustom, calls=%fused_computation | custom fusion | bytes 5263360 | tf_op jit(solution)/shard_map/jit(_take)/gather | solution.py:51
  79.8 4.2 %select_bitcast_fusion.1 = f32[128,5120]{0,1:T(8,128)S(1)} fusion(f32[5120,128]{1,0:T(8,128)} %gather_fusion, pred[5120]{0:T(1024)(128)(4,1)S(1)} %compare_and_fusion), kind=kLoop, calls=%fused_computation.7 | loop fusion | flops 655360 | bytes 5248000 | tf_op jit(solution)/shard_map/jit(_take)/select_n | solution.py:51
  84.1 10.8 %convolution_bitcast_fusion.1 = f32[128]{0:T(128)S(1)} fusion(f32[128,20480]{1,0:T(8,128)} %param.12, f32[20480,1]{0,1:T(1,128)S(1)} %bitcast.64), kind=kOutput, calls=%fused_computation.9 | convolution fusion | flops 31457280 | bytes 10568192 | tf_op jit(solution)/shard_map/dot_general | solution.py:53
  111.8 33.6 %all-gather.7.cloned.1.call-done = f32[64,4,20480]{2,1,0:T(4,128)} async-done(((f32[1,4,20480]{2,1,0:T(4,128)}), f32[64,4,20480]{2,1,0:T(4,128)}) %all-gather.7.cloned.1.call-update) | async-done | bytes 20971536 | tf_op jit(solution)/shard_map/all_gather | solution.py:37
  145.4 10.8 %reduce_sum.9 = f32[4,20480]{1,0:T(4,128)S(1)} reduce(f32[64,4,20480]{2,1,0:T(4,128)} %all-gather.7.cloned.1.call-done, f32[]{:T(128)} %constant.115.clone.1), dimensions={0}, to_apply=%region_0.1 | reduce | flops 5160960 | bytes 21299204 | tf_op jit(solution)/shard_map/reduce_sum | solution.py:37
  156.3 5.6 %copy.24 = f32[4,20480]{0,1:T(8,128)} copy(f32[4,20480]{1,0:T(4,128)S(1)} %reduce_sum.9) | data formatting | bytes 655360 | tf_op jit(solution)/shard_map/reduce_sum | solution.py:37
  190.2 21.7 %gather_fusion.1 = f32[5120,4]{1,0:T(8,128)} fusion(f32[4,20480]{0,1:T(8,128)} %copy.24, s32[5120]{0:T(1024)S(1)} %broadcast_clamp_fusion), kind=kCustom, calls=%fused_computation.1 | custom fusion | bytes 184320 | tf_op jit(solution)/shard_map/jit(_take)/gather | solution.py:51
  212.5 1.1 multiply_subtract_fusion.4
  213.6 1.5 convolution_bitcast_fusion
  215.1 5.3 %select_bitcast_fusion = f32[4,5120]{0,1:T(8,128)} fusion(f32[5120,4]{1,0:T(8,128)} %gather_fusion.1, pred[5120]{0:T(1024)(128)(4,1)S(1)} %compare_and_fusion), kind=kLoop, calls=%fused_computation.6 | loop fusion | flops 20480 | bytes 168960 | tf_op jit(solution)/shard_map/jit(_take)/select_n | solution.py:51
  220.5 1.0 pad_maximum_fusion
  221.5 10.1 %all-gather.5.cloned.1.call-done = f32[5120,512]{1,0:T(8,128)} async-done(((f32[80,512]{1,0:T(8,128)}), f32[5120,512]{1,0:T(8,128)}) %all-gather.5.cloned.1.call-update) | async-done | bytes 10485776 | tf_op jit(solution)/shard_map/all_gather | solution.py:48
  231.7 20.4 %fusion = f32[132,512]{1,0:T(8,128)S(1)} fusion(f32[5120,512]{1,0:T(8,128)} %all-gather.5.cloned.1.call-done, f32[4,5120]{0,1:T(8,128)} %select_bitcast_fusion, f32[128,5120]{0,1:T(8,128)S(1)} %select_bitcast_fusion.1), kind=kOutput, calls=%fused_computation.2 | convolution fusion | flops 4153036800 | bytes 13459456 | tf_op jit(solution)/shard_map/dot_general | solution.py:95
  255.7 1.2 fusion.8
  256.9 0.9 fusion.7
  (43 shorter events, 12.2 us)
Async XLA Ops:
  7.2 76.9 %copy-start = (f32[20480]{0:T(1024)S(1)}, f32[20480]{0:T(1024)}, u32[]{:S(2)}) copy-start(f32[20480]{0:T(1024)} %param.17) | copy-start | bytes 245764
  7.2 138.2 %all-gather.7.cloned.1.call-start = ((), (), s32[]{:S(2)}) async-start(), calls=%async_computation.2 | async-start | bytes 21299200 | tf_op jit(solution)/shard_map/all_gather | solution.py:37
  39.9 71.2 %all-to-all-start = ((f32[20,4,512]{2,0,1:T(8,128)}), f32[20,4,512]{2,0,1:T(8,128)S(1)}, u32[]{:S(2)}, u32[]{:S(2)}) async-start(f32[20,4,512]{2,0,1:T(8,128)} %copy.25), calls=%async_computation | async-start | bytes 393216 | tf_op jit(solution)/shard_map/all_to_all | solution.py:47
  44.7 187.0 %all-gather.5.cloned.1.call-start = ((), (), s32[]{:S(2)}) async-start(), calls=%async_computation.1 | async-start | bytes 10649600 | tf_op jit(solution)/shard_map/all_gather | solution.py:48
  84.0 10.8 %copy-start.1 = (s32[4,2]{0,1:T(2,128)S(1)}, s32[4,2]{0,1:T(2,128)}, u32[]{:S(2)}) copy-start(s32[4,2]{0,1:T(2,128)} %param.20) | copy-start | bytes 100
  84.0 26.3 %copy-start.3 = (f32[4]{0:T(128)S(1)}, f32[4]{0:T(128)}, u32[]{:S(2)}) copy-start(f32[4]{0:T(128)} %param.23) | copy-start | bytes 52
  221.5 30.5 %copy-start.2 = (f32[512]{0:T(512)S(1)}, f32[512]{0:T(512)}, u32[]{:S(2)}) copy-start(f32[512]{0:T(512)} %param.18) | copy-start | bytes 6148
Sparse Core Ops, SparseCore 0:
  31.2 114.1 all-gather.6
  148.7 82.9 all-gather.4
